TPU v7x, 256 devices: a whole 4x4x8 slice. The times are simulated.
256 devices in a mesh: svc: 32 (over y_lo, z, core), tm: 8 (over y_hi, x).
Axes of the slice: x: 4, y: 4 (y_hi: 2, y_lo: 2; y = y_hi * 2 + y_lo), z: 8, core: 2. Of those that a mesh axis runs over, the one named last changes fastest.
Arguments:
- metrics: bfloat16 [8192, 4096], P('svc', 'tm'), may hold values from -15 to 15
- band_starts: int32 [4], replicated, may hold values from 1 to 2015
Outputs:
- cross: bfloat16 [4, 2, 8192, 8192], P(None, None, 'svc', 'tm')
- coherence: float32 [4, 8192, 8192], P(None, 'svc', 'tm')
Inputs may be any that keep to these rules, and one draw needn't show every extreme that they name: `band_starts`: each band covers 32 consecutive bins starting at its entry.
All inputs are finite; a program needn't handle non-finite values.
Results may differ from a plain program's by a relative error of at most 0.0066.
Values may be sent and summed in bfloat16 or wider, within the bound.
No kernel may reach another device: no remote copies, remote signals or barrier semaphores. Data moves between devices by JAX's collectives and lax.ppermute only.
A program may use at most 64 MiB of HBM per device.

v0:
```python
import jax
import jax.numpy as jnp
from jax import lax
from jax.sharding import PartitionSpec as P

TLEN = 4096
BANDS = 4
BINS = 32
epsilon = 1e-06


def make_table(minutes, band_starts):
    offsets = jnp.arange(BINS, dtype=jnp.int32)
    freqs = band_starts[:, None] + offsets[None, :]
    phase_index = minutes[:, None, None] * freqs[None, :, :] % TLEN
    phases = 2.0 * jnp.pi / TLEN * phase_index.astype(jnp.float32)
    norm = 1.0 / jnp.sqrt(jnp.float32(TLEN))
    stacked = jnp.stack([jnp.cos(phases) * norm, -jnp.sin(phases) * norm], axis=2)
    return stacked.reshape(minutes.shape[0], BANDS * 2 * BINS).astype(jnp.bfloat16)


def band_products(row_spec, col_spec):
    swapped = jnp.concatenate([row_spec[:, BINS:], -row_spec[:, :BINS]], axis=1)
    dims = (((1,), (1,)), ((), ()))
    real_part = lax.dot_general(row_spec, col_spec, dims, preferred_element_type=jnp.float32) / BINS
    imag_part = lax.dot_general(swapped, col_spec, dims, preferred_element_type=jnp.float32) / BINS
    row_power = jnp.sum(jnp.square(row_spec.astype(jnp.float32)), axis=1) / BINS
    col_power = jnp.sum(jnp.square(col_spec.astype(jnp.float32)), axis=1) / BINS
    coherence = (real_part * real_part + imag_part * imag_part) / (
        (row_power[:, None] + epsilon) * (col_power[None, :] + epsilon)
    )
    cross = jnp.stack([real_part, imag_part], axis=0).astype(jnp.bfloat16)
    return (cross, coherence)


def body(metrics, band_starts):
    row_count = metrics.shape[0]
    local_minutes = metrics.shape[1]
    n_tm = lax.axis_size("tm")
    n_svc = lax.axis_size("svc")
    owners = n_svc // n_tm
    width = BANDS * 2 * BINS
    chunk = width // n_tm
    time_index = lax.axis_index("tm")
    minutes = time_index * local_minutes + jnp.arange(local_minutes, dtype=jnp.int32)
    dft_table = make_table(minutes, band_starts).reshape(local_minutes, n_tm, chunk)
    partial_value = jnp.einsum(
        "nt,tcb->cnb", metrics, dft_table, preferred_element_type=jnp.float32
    )
    piece = lax.psum_scatter(partial_value, "tm", scatter_dimension=0, tiled=True)
    piece = piece.astype(jnp.bfloat16)
    row_chunks = lax.all_gather(piece, "tm", axis=0, tiled=True)
    spectra = jnp.transpose(row_chunks, (1, 0, 2)).reshape(row_count, width)
    perm = []
    for s_src in range(n_svc):
        g_src, r_src = divmod(s_src, owners)
        for t_src in range(n_tm):
            s_dst = t_src * owners + r_src
            t_dst = g_src
            perm.append((s_src * n_tm + t_src, s_dst * n_tm + t_dst))
    moved = lax.ppermute(piece, ("svc", "tm"), perm)
    col_chunks = lax.all_gather(moved, "svc", axis=0, tiled=True)
    columns_panel = (
        col_chunks.reshape(n_tm, owners, row_count, chunk)
        .transpose(1, 2, 0, 3)
        .reshape(owners * row_count, width)
    )
    cross_list = []
    coherence_list = []
    for band in range(BANDS):
        offset = band * 2 * BINS
        row_spec = spectra[:, offset : offset + 2 * BINS]
        col_spec = columns_panel[:, offset : offset + 2 * BINS]
        cross, coherence = band_products(row_spec, col_spec)
        cross_list.append(cross)
        coherence_list.append(coherence)
    return (jnp.stack(cross_list, axis=0), jnp.stack(coherence_list, axis=0))


def solution(mesh):
    return jax.shard_map(
        body,
        mesh=mesh,
        in_specs=(P("svc", "tm"), P()),
        out_specs=(P(None, None, "svc", "tm"), P(None, "svc", "tm")),
        check_vma=False,
    )
```

profile of v0, /device:TPU:1, one launch (start us, length us, event | category | flops | bytes accessed | tf_op | source)
XLA Modules:
  0.0 182.2 jit_solution(15294440074042725612)
XLA Ops:
  7.2 0.0 copy-start
  7.2 0.0 reduce-scatter.2.cloned.1.call-start
  7.2 0.8 iota_add_fusion
  8.0 1.2 multiply_convert_fusion.1
  9.3 0.0 copy-done
  9.3 1.0 convolution_bitcast_fusion
  10.2 0.0 reduce-scatter.2.cloned.1.call-update
  10.3 79.3 %reduce-scatter.2.cloned.1.call-done = f32[1,256,32]{1,2,0:T(8,128)} async-done(((f32[8,256,32]{1,2,0:T(8,128)}), f32[1,256,32]{1,2,0:T(8,128)}) %reduce-scatter.2.cloned.1.call-update) | async-done | bytes 32784 | tf_op jit(solution)/shard_map/reduce_scatter | solution.py:50
  89.6 0.8 convert_element_type.80
  90.3 0.7 collective-permute-start
  91.0 34.3 %all_gather.6 = bf16[8,256,32]{1,2,0:T(8,128)(2,1)S(1)} all-gather(bf16[1,256,32]{1,2,0:T(8,128)(2,1)S(1)} %convert_element_type.80), channel_id=1, replica_groups=mesh['svc'=32,'tm'=8] {'tm'}, dimensions={0}, use_global_device_ids=true | all-gather | bytes 147456 | tf_op jit(solution)/shard_map/all_gather | solution.py:52
  125.4 0.0 collective-permute-done
  125.4 41.4 %all_gather.7 = bf16[32,256,32]{1,2,0:T(8,128)(2,1)S(1)} all-gather(bf16[1,256,32]{1,2,0:T(8,128)(2,1)S(1)} %collective-permute-done), channel_id=1, replica_groups=mesh['svc'=32,'tm'=8] {'svc'}, dimensions={0}, use_global_device_ids=true | all-gather | bytes 540672 | tf_op jit(solution)/shard_map/all_gather | solution.py:62
  166.8 0.4 copy.5
  167.2 0.1 copy.6
  167.3 0.1 multiply_reduce_fusion.3
  167.5 0.3 convolution_multiply_fusion.6
  167.8 0.3 convolution_multiply_fusion.2
  168.1 0.3 convolution_multiply_fusion
  168.4 0.3 convolution_multiply_fusion.4
  168.8 0.4 divide_bitcast_fusion.2
  169.2 0.4 divide_bitcast_fusion
  169.6 0.4 divide_bitcast_fusion.1
  170.1 0.4 divide_bitcast_fusion.3
  170.5 2.3 %pad_maximum_fusion = f32[4,256,1024]{2,1,0:T(8,128)} fusion(f32[1,256,1024]{2,1,0:T(8,128)S(1)} %get-tuple-element.19, f32[1,256,1024]{2,1,0:T(8,128)S(1)} %get-tuple-element.16, f32[1,256,1024]{2,1,0:T(8,128)S(1)} %get-tuple-element.13, f32[1,256,1024]{2,1,0:T(8,128)S(1)} %get-tuple-element.10), kind=kLoop, calls=%fused_computation.1 | loop fusion | flops 3145728 | bytes 8388608 | tf_op jit(solution)/shard_map/stack | solution.py:77
  172.8 2.6 %maximum_maximum_fusion = bf16[4,2,256,1024]{3,2,1,0:T(8,128)(2,1)} fusion(bf16[1,1,256,1024]{3,2,1,0:T(8,128)(2,1)S(1)} %get-tuple-element.21, bf16[1,1,256,1024]{3,2,1,0:T(8,128)(2,1)S(1)} %get-tuple-element.20, bf16[1,1,256,1024]{3,2,1,0:T(8,128)(2,1)S(1)} %get-tuple-element.18, bf16[1,1,256,1024]{3,2,1,0:T(8,128)(2,1)S(1)} %get-tuple-element.17, ...), kind=kLoop, calls=%fused_computation | loop fusion | flops 14680064 | bytes 8388608 | tf_op jit(solution)/shard_map/stack | solution.py:77
  (8 shorter events, 0.1 us)
Async XLA Ops:
  7.2 2.1 %copy-start = (bf16[256,512]{1,0:T(8,128)(2,1)S(1)}, bf16[256,512]{1,0:T(8,128)(2,1)}, u32[]{:S(2)}) copy-start(bf16[256,512]{1,0:T(8,128)(2,1)} %param.2) | copy-start | bytes 786436
  7.2 82.4 %reduce-scatter.2.cloned.1.call-start = ((), (), s32[]{:S(2)}) async-start(), calls=%async_computation.1 | async-start | bytes 294912 | tf_op jit(solution)/shard_map/reduce_scatter | solution.py:50
  90.3 35.0 %collective-permute-start = (bf16[1,256,32]{1,2,0:T(8,128)(2,1)S(1)}, bf16[1,256,32]{1,2,0:T(8,128)(2,1)S(1)}, u32[]{:S(2)}, u32[]{:S(2)}) collective-permute-start(bf16[1,256,32]{1,2,0:T(8,128)(2,1)S(1)} %convert_element_type.80), channel_id=1, source_target_pairs={{0,0},{1,32},{2,64},{3,96},{4,128},{5,160},{6,192},{7,224},{8,8},{... | collective-permute-start | bytes 49160 | tf_op jit(solution)/shard_map/ppermute | solution.py:61
Sparse Core Ops, SparseCore 0:
  12.4 77.0 reduce-scatter.1
where the time goes:
time: 182 us
  waiting for transfers between devices  79.3 us (44%)
  blocking collectives  75.7 us (42%)
  between operations  14.2 us (8%)
  other arithmetic  7.89 us (4%)
  matrix products  3.91 us (2%)
    reduce_scatter x1, waiting for transfers between devices, body(): lax.psum_scatter(partial_value, 'tm', scatter_dimension=0, tiled=True)  79.3 us
    all_gather x1, blocking collectives, body(): col_chunks = lax.all_gather(moved, 'svc', axis=0, tiled=True)  41.4 us
    all_gather x1, blocking collectives, body(): row_chunks = lax.all_gather(piece, 'tm', axis=0, tiled=True)  34.3 us
    another operation x2, other arithmetic, body(): return (jnp.stack(cross_list, axis=0), jnp.stack(coherence_list, axis=0))  4.9 us
  transfers between devices with their start and end apart: 2, of which 1 were waited for; matrix products, arithmetic and copies ran while one was open for 0% of the time, Pallas kernels for 0%

commit v1 on v0

--- a/solution.py
+++ b/solution.py
@@ -49,7 +49,9 @@
     )
     piece = lax.psum_scatter(partial_value, "tm", scatter_dimension=0, tiled=True)
     piece = piece.astype(jnp.bfloat16)
-    row_chunks = lax.all_gather(piece, "tm", axis=0, tiled=True)
+    row_chunks = jnp.concatenate(
+        lax.all_to_all(jnp.stack([piece] * lax.axis_size("tm")), "tm", 0, 0), axis=0
+    )
     spectra = jnp.transpose(row_chunks, (1, 0, 2)).reshape(row_count, width)
     perm = []
     for s_src in range(n_svc):

time: 182 us -> 156 us (0.86)
  blocking collectives: 75.7 us -> 35.4 us
  starting transfers between devices: 0.69 us -> 13.2 us
    all_gather x1 -> x0, blocking collectives: 34.3 us -> none  [body(): row_chunks = lax.all_gather(piece, 'tm', axis=0, tiled=True)]
    all_to_all x0 -> x1, starting transfers between devices: none -> 12.5 us  [body(): lax.all_to_all(jnp.stack([piece] * lax.axis_size('tm')), 'tm', 0, 0)]
    all_gather x1, blocking collectives: 41.4 us -> 35.4 us  [body(): col_chunks = lax.all_gather(moved, 'svc', axis=0, tiled=True)]
  transfers between devices with their start and end apart: 2 -> 3, of which waited for: 1 -> 1; matrix products, arithmetic and copies ran while one was open for 0% -> 1% of each run, Pallas kernels for 0% -> 0%
where the time goes in v1:
time: 156 us
  waiting for transfers between devices  79.3 us (51%)
  blocking collectives  35.4 us (23%)
  between operations  14.2 us (9%)
  starting transfers between devices  13.2 us (8%)
  other arithmetic  8.65 us (6%)
  matrix products  3.91 us (3%)
    reduce_scatter x1, waiting for transfers between devices, body(): lax.psum_scatter(partial_value, 'tm', scatter_dimension=0, tiled=True)  79.3 us
    all_gather x1, blocking collectives, body(): col_chunks = lax.all_gather(moved, 'svc', axis=0, tiled=True)  35.4 us
    all_to_all x1, starting transfers between devices, body(): lax.all_to_all(jnp.stack([piece] * lax.axis_size('tm')), 'tm', 0, 0)  12.5 us
    another operation x2, other arithmetic, body(): return (jnp.stack(cross_list, axis=0), jnp.stack(coherence_list, axis=0))  4.9 us
  transfers between devices with their start and end apart: 3, of which 1 were waited for; matrix products, arithmetic and copies ran while one was open for 1% of the time, Pallas kernels for 0%

profile of v1, /device:TPU:1, one launch (start us, length us, event | category | flops | bytes accessed | tf_op | source)
XLA Modules:
  0.0 155.9 jit_solution(6283673054088697534)
XLA Ops:
  7.2 0.0 copy-start
  7.2 0.0 reduce-scatter.2.cloned.1.call-start
  7.2 0.8 iota_add_fusion
  8.0 1.2 multiply_convert_fusion.1
  9.3 0.0 copy-done
  9.3 1.0 convolution_bitcast_fusion
  10.2 0.0 reduce-scatter.2.cloned.1.call-update
  10.3 79.3 %reduce-scatter.2.cloned.1.call-done = f32[1,256,32]{1,2,0:T(8,128)} async-done(((f32[8,256,32]{1,2,0:T(8,128)}), f32[1,256,32]{1,2,0:T(8,128)}) %reduce-scatter.2.cloned.1.call-update) | async-done | bytes 32784 | tf_op jit(solution)/shard_map/reduce_scatter | solution.py:50
  89.6 0.8 convert_element_type.82
  90.3 0.7 collective-permute-start
  91.0 0.8 convert_bitcast_fusion.8
  91.8 0.7 stack.76
  92.4 12.5 %all-to-all-start = ((bf16[8,1,256,32]{2,3,1,0:T(8,128)(2,1)}), bf16[8,1,256,32]{2,3,1,0:T(8,128)(2,1)S(1)}, u32[]{:S(2)}, u32[]{:S(2)}) async-start(bf16[8,1,256,32]{2,3,1,0:T(8,128)(2,1)} %stack.76), calls=%async_computation.1 | async-start | bytes 262144 | tf_op jit(solution)/shard_map/all_to_all | solution.py:53
  104.9 0.0 collective-permute-done
  104.9 35.4 %all_gather.3 = bf16[32,256,32]{1,2,0:T(8,128)(2,1)S(1)} all-gather(bf16[1,256,32]{1,2,0:T(8,128)(2,1)S(1)} %collective-permute-done), channel_id=1, replica_groups=mesh['svc'=32,'tm'=8] {'svc'}, dimensions={0}, use_global_device_ids=true | all-gather | bytes 540672 | tf_op jit(solution)/shard_map/all_gather | solution.py:64
  140.3 0.4 copy.6
  140.7 0.1 copy.7
  140.8 0.1 multiply_reduce_fusion.3
  141.0 0.0 all-to-all-done
  141.1 0.3 convolution_multiply_fusion.6
  141.4 0.3 convolution_multiply_fusion.2
  141.7 0.3 convolution_multiply_fusion
  142.1 0.3 convolution_multiply_fusion.4
  142.4 0.4 divide_bitcast_fusion.2
  142.8 0.4 divide_bitcast_fusion
  143.2 0.4 divide_bitcast_fusion.1
  143.7 0.4 divide_bitcast_fusion.3
  144.1 2.3 %pad_maximum_fusion = f32[4,256,1024]{2,1,0:T(8,128)} fusion(f32[1,256,1024]{2,1,0:T(8,128)S(1)} %get-tuple-element.19, f32[1,256,1024]{2,1,0:T(8,128)S(1)} %get-tuple-element.16, f32[1,256,1024]{2,1,0:T(8,128)S(1)} %get-tuple-element.13, f32[1,256,1024]{2,1,0:T(8,128)S(1)} %get-tuple-element.10), kind=kLoop, calls=%fused_computation.1 | loop fusion | flops 3145728 | bytes 8388608 | tf_op jit(solution)/shard_map/stack | solution.py:79
  146.4 2.6 %maximum_maximum_fusion = bf16[4,2,256,1024]{3,2,1,0:T(8,128)(2,1)} fusion(bf16[1,1,256,1024]{3,2,1,0:T(8,128)(2,1)S(1)} %get-tuple-element.21, bf16[1,1,256,1024]{3,2,1,0:T(8,128)(2,1)S(1)} %get-tuple-element.20, bf16[1,1,256,1024]{3,2,1,0:T(8,128)(2,1)S(1)} %get-tuple-element.18, bf16[1,1,256,1024]{3,2,1,0:T(8,128)(2,1)S(1)} %get-tuple-element.17, ...), kind=kLoop, calls=%fused_computation | loop fusion | flops 14680064 | bytes 8388608 | tf_op jit(solution)/shard_map/stack | solution.py:79
  (8 shorter events, 0.1 us)
Async XLA Ops:
  7.2 2.1 %copy-start = (bf16[256,512]{1,0:T(8,128)(2,1)S(1)}, bf16[256,512]{1,0:T(8,128)(2,1)}, u32[]{:S(2)}) copy-start(bf16[256,512]{1,0:T(8,128)(2,1)} %param.2) | copy-start | bytes 786436
  7.2 82.4 %reduce-scatter.2.cloned.1.call-start = ((), (), s32[]{:S(2)}) async-start(), calls=%async_computation.2 | async-start | bytes 294912 | tf_op jit(solution)/shard_map/reduce_scatter | solution.py:50
  90.3 14.6 %collective-permute-start = (bf16[1,256,32]{1,2,0:T(8,128)(2,1)S(1)}, bf16[1,256,32]{1,2,0:T(8,128)(2,1)S(1)}, u32[]{:S(2)}, u32[]{:S(2)}) collective-permute-start(bf16[1,256,32]{1,2,0:T(8,128)(2,1)S(1)} %convert_element_type.82), channel_id=1, source_target_pairs={{0,0},{1,32},{2,64},{3,96},{4,128},{5,160},{6,192},{7,224},{8,8},{... | collective-permute-start | bytes 49160 | tf_op jit(solution)/shard_map/ppermute | solution.py:63
  92.4 48.6 %all-to-all-start = ((bf16[8,1,256,32]{2,3,1,0:T(8,128)(2,1)}), bf16[8,1,256,32]{2,3,1,0:T(8,128)(2,1)S(1)}, u32[]{:S(2)}, u32[]{:S(2)}) async-start(bf16[8,1,256,32]{2,3,1,0:T(8,128)(2,1)} %stack.76), calls=%async_computation.1 | async-start | bytes 262144 | tf_op jit(solution)/shard_map/all_to_all | solution.py:53
Sparse Core Ops, SparseCore 0:
  12.4 77.0 reduce-scatter.1
